TPU v7x, 512 devices: a whole 4x8x8 slice. The times are simulated.
512 devices in a mesh: band: 128 (over x, z_hi, y, core), depth: 4 (over z_lo).
Axes of the slice: x: 4, y: 8, z: 8 (z_hi: 2, z_lo: 4; z = z_hi * 4 + z_lo), core: 2. Of those that a mesh axis runs over, the one named last changes fastest.
Arguments:
- orbitals: bfloat16 [128, 32, 128, 128], P('band', 'depth'), may hold values from -6 to 6
- dielectric: float32 [32, 128, 128], P('depth'), may hold values from 1 to 4
- occupied: int32 [128], P('band'), may hold values 0 or 1
- plan: int32 [2, 128, 1], P(None, 'band'), may hold values 0 or 1
Outputs:
- exchange: float32 [128, 32, 128, 128], P('band', 'depth')
All inputs are finite; a program needn't handle non-finite values. No bound on the sum of `occupied` or of `plan` on one device may be relied on, other than what follows from the above.
Results may differ from a plain program's by a relative error of at most 0.0003.
Values may be sent and summed in bfloat16 or wider, within the bound.
No kernel may reach another device: no remote copies, remote signals or barrier semaphores. Data moves between devices by JAX's collectives and lax.ppermute only.
A program may use at most 64 MiB of HBM per device.

v0:
```python
import functools
import math

import jax
import jax.numpy as jnp
from jax import lax
from jax.experimental import pallas as pl
from jax.experimental.pallas import tpu as pltpu
from jax.sharding import PartitionSpec as P


SWEEPS = 2


FOUR_PI = 4.0 * math.pi
KAPPA_SQ = 4.0
CHEB_CENTER = 28.0
CHEB_HALF = 24.0
HALO = SWEEPS


def shifted(x, axis, by):
    size = lax.axis_size(axis)
    return lax.ppermute(x, axis, [(i, (i + by) % size) for i in range(size)])


def z_halo(x, dim, width):
    length = x.shape[dim]
    last = lax.slice_in_dim(x, length - width, length, axis=dim)
    leading = lax.slice_in_dim(x, 0, width, axis=dim)
    before = shifted(last, "depth", 1)
    after = shifted(leading, "depth", -1)
    return jnp.concatenate([before, x, after], axis=dim)


def solve_kernel(windows, sources, weight_ref, psi_ref, eps_ref, *refs):
    if sources is None:
        middle_ref, kept_second, kept_rem, kept_partial, out_ref = refs[:5]
        weights_out = None
        scratch = refs[5:]
    else:
        middle_ref = None
        out_ref, weights_out, kept_second, kept_rem, kept_partial = refs[:5]
        scratch = refs[5:]
    face_z, face_x, face_y, dens, first, rem, second, partial, flux = scratch
    _, rows, cols = eps_ref.shape
    pairs = psi_ref.shape[0] - 1

    if sources is not None:
        odd = weight_ref[0]
        for k, (tick, own_when_odd) in enumerate(sources):
            own = weight_ref[1 + tick]
            pick = odd if own_when_odd else 1.0 - odd
            sent = psi_ref[k + 1, pl.ds(sources_row(psi_ref) + tick, 1), :].astype(jnp.float32)
            weights_out[k] = pick * own + (1.0 - pick) * sent
        weight_of = weights_out
    else:
        weight_of = weight_ref

    def layer(slab, e):
        if len(psi_ref.shape) == 4:
            return psi_ref[slab, e].astype(jnp.float32)
        return psi_ref[slab, pl.ds(pl.multiple_of(e * rows, rows), rows), :].astype(jnp.float32)

    def applied(field, e):
        center = field[e]
        flux_up = face_z[e] * (field[e + 1] - center)
        flux_down = flux[...]
        flux[...] = flux_up
        part_z = flux_up - flux_down
        flux_x = face_x[e] * (pltpu.roll(center, rows - 1, 0) - center)
        part_x = flux_x - pltpu.roll(flux_x, 1, 0)
        flux_y = face_y[e] * (pltpu.roll(center, cols - 1, 1) - center)
        part_y = flux_y - pltpu.roll(flux_y, 1, 1)
        return KAPPA_SQ * center - (part_z + part_x + part_y)

    sigma = CHEB_CENTER / CHEB_HALF
    factor = CHEB_HALF / CHEB_CENTER
    factor_one = 1.0 / (2.0 * sigma - factor)
    factor_two = 1.0 / (2.0 * sigma - factor_one)
    keep_one, mix_one = factor_one * factor, 2.0 * factor_one / CHEB_HALF
    keep_two, mix_two = factor_two * factor_one, 2.0 * factor_two / CHEB_HALF

    for start, size, at, dens_span, sweep_span, taken in windows:
        count = size - 2 * HALO
        out_ref[pl.ds(at, count)] = jnp.zeros((count, rows, cols), out_ref.dtype)

        def faces(e, carry):
            cur = eps_ref[start + e]
            face_x[e] = (cur + pltpu.roll(cur, rows - 1, 0)) * 0.5
            face_y[e] = (cur + pltpu.roll(cur, cols - 1, 1)) * 0.5
            face_z[e] = (cur + eps_ref[start + e + 1]) * 0.5
            return carry

        lax.fori_loop(0, size - 1, faces, 0)

        for k in range(pairs):
            weight = weight_of[k]

            def density(e, carry):
                value = (FOUR_PI * layer(0, start + e)) * layer(k + 1, start + e)
                dens[e] = value
                first[e] = value / CHEB_CENTER
                return carry

            lax.fori_loop(dens_span[0], dens_span[1], density, 0)

            def sweep_one(e, carry):
                center = first[e]
                remainder = dens[e] - applied(first, e)
                direction = keep_one * center + mix_one * remainder
                rem[e] = remainder
                second[e] = direction
                partial[e] = center + direction
                return carry

            lo, hi = sweep_span
            flux[...] = face_z[lo - 1] * (first[lo] - first[lo - 1])
            lax.fori_loop(lo, hi, sweep_one, 0)
            if sources is not None:
                for j, e in enumerate((1, 2, size - 3, size - 2)):
                    kept_second[k, j] = second[e]
                for j, e in enumerate((1, size - 2)):
                    kept_rem[k, j] = rem[e]
                    kept_partial[k, j] = partial[e]
            else:
                seconds, both = taken
                for e, j in seconds:
                    second[e] = kept_second[k, j]
                e, j = both
                rem[e] = kept_rem[k, j]
                partial[e] = kept_partial[k, j]

            def sweep_two(e, carry):
                remainder = rem[e] - applied(second, e)
                direction = keep_two * second[e] + mix_two * remainder
                potential = partial[e] + direction
                out_ref[at + e - HALO] += (weight * potential) * layer(k + 1, start + e)
                return carry

            flux[...] = face_z[1] * (second[2] - second[1])
            lax.fori_loop(HALO, size - HALO, sweep_two, 0)
        out_ref[pl.ds(at, count)] = -out_ref[pl.ds(at, count)]
    if middle_ref is not None:
        out_ref[pl.ds(HALO, middle_ref.shape[0])] = middle_ref[...]


def sources_row(psi_ref):
    return psi_ref.shape[1] - 16


def solve(weights, psi, eps, windows, outputs, sources=None, middle=None, kept=None):
    rows, cols = eps.shape[1:]
    pairs = psi.shape[0] - 1
    widest = max(window[1] for window in windows)
    work = sum(3 * window[1] for window in windows)
    vmem = pltpu.VMEM
    layer = (rows, cols)
    kept_shapes = [
        jax.ShapeDtypeStruct((pairs, 4) + layer, jnp.float32),
        jax.ShapeDtypeStruct((pairs, 2) + layer, jnp.float32),
        jax.ShapeDtypeStruct((pairs, 2) + layer, jnp.float32),
    ]
    out_shape = [jax.ShapeDtypeStruct((outputs,) + layer, jnp.float32)]
    operands = [weights, psi, eps]
    in_specs = [pl.BlockSpec(memory_space=pltpu.SMEM if sources is not None else vmem), pl.BlockSpec(memory_space=vmem), pl.BlockSpec(memory_space=vmem)]
    if sources is not None:
        out_shape += [jax.ShapeDtypeStruct((pairs, 1, cols), jnp.float32)] + kept_shapes
    else:
        operands += [middle] + list(kept)
        in_specs += [pl.BlockSpec(memory_space=vmem)] * 4
    return pl.pallas_call(
        functools.partial(solve_kernel, tuple(windows), sources),
        out_shape=tuple(out_shape),
        in_specs=in_specs,
        out_specs=tuple(pl.BlockSpec(memory_space=vmem) for _ in out_shape),
        scratch_shapes=[vmem((widest,) + layer, jnp.float32)] * 8 + [vmem(layer, jnp.float32)],
        compiler_params=pltpu.CompilerParams(vmem_limit_bytes=48 * 1024 * 1024),
        cost_estimate=pl.CostEstimate(
            flops=pairs * work * rows * cols * 25,
            transcendentals=0,
            bytes_accessed=psi.size * 2 + eps.size * 4 + outputs * rows * cols * 4,
        ),
    )(*operands)


def exchanged(x, axis, pairs_of):
    size = lax.axis_size(axis)
    return lax.ppermute(x, axis, [(i, pairs_of(i) % size) for i in range(size)])


def on_device(orbitals, dielectric, occupied, plan):
    psi = orbitals[0]
    depth, rows, cols = psi.shape
    ticks = plan.shape[0]
    flags = plan.astype(jnp.float32).reshape(ticks)
    padded_diel = z_halo(dielectric, 0, HALO)

    info = jnp.zeros((16, cols), jnp.bfloat16).at[:ticks, :].set(
        jnp.broadcast_to(plan.astype(jnp.bfloat16).reshape(ticks, 1), (ticks, cols))
    )
    message = jnp.concatenate(
        [(psi * occupied.astype(jnp.bfloat16)[0]).reshape(depth * rows, cols), info], axis=0
    )
    outer = exchanged(message, "band", lambda b: b + 1 if b % 2 else b - 1)
    far = exchanged(message, "band", lambda b: b - 2 if b % 2 else b + 2)
    both = exchanged(jnp.stack([message, outer]), "band", lambda b: b ^ 1)
    swap, relay = both[0], both[1]

    sources = ((0, True), (0, False), (1, False), (1, True))
    odd = (lax.axis_index("band") % 2).astype(jnp.float32)
    scalars = jnp.concatenate([odd[None], flags])
    own = jnp.concatenate([psi.reshape(depth * rows, cols), info], axis=0)
    stack = jnp.stack([own, swap, outer, far, relay])
    inner, weights, *kept = solve(
        scalars, stack, dielectric, [(0, depth, 0, (0, depth), (1, depth - 1), None)], depth - 2 * HALO, sources=sources
    )
    layers = stack[:, : depth * rows].reshape(stack.shape[0], depth, rows, cols)
    wide = z_halo(layers, 1, HALO)
    windows = [
        (0, 3 * HALO, 0, (0, 4), (1, 3), (((3, 0), (4, 1)), (3, 0))),
        (depth - HALO, 3 * HALO, depth - HALO, (2, 6), (3, 5), (((1, 2), (2, 3)), (2, 1))),
    ]
    (totals,) = solve(weights, wide, padded_diel, windows, depth, middle=inner, kept=kept)
    return totals[None]


def solution(mesh):
    placed = (
        P("band", "depth", None, None),
        P("depth", None, None),
        P("band"),
        P(None, "band", None),
    )

    return jax.shard_map(
        on_device,
        mesh=mesh,
        in_specs=placed,
        out_specs=P("band", "depth", None, None),
        check_vma=False,
    )
```

profile of v0, /device:TPU:64, one launch (start us, length us, event | category | flops | bytes accessed | tf_op | source)
XLA Modules:
  0.0 86.7 jit_solution(13310218715166384260)
XLA Ops:
  0.0 0.0 copy-start.1
  0.0 0.7 convert_bitcast_fusion
  1.4 1.0 %broadcast_multiply_fusion = bf16[1024,128]{1,0:T(8,128)(2,1)S(1)} fusion(bf16[]{:T(256)} %bitcast.5, bf16[1,8,128,128]{3,2,1,0:T(8,128)(2,1)} %param.6), kind=kLoop, calls=%fused_computation.9 | loop fusion | flops 131072 | bytes 524290 | tf_op jit(solution)/shard_map/mul | solution.py:203
  2.4 0.2 fusion.2
  2.6 14.6 %collective-permute-start = (bf16[1040,128]{1,0:T(8,128)(2,1)S(1)}, bf16[1040,128]{1,0:T(8,128)(2,1)S(1)}, u32[]{:S(2)}, u32[]{:S(2)}) collective-permute-start(bf16[1040,128]{1,0:T(8,128)(2,1)S(1)} %get-tuple-element.32), channel_id=1, source_target_pairs={{0,508},{4,8},{8,4},{12,16},{16,12},{20,24},{24,20},{28,32},{32,28... | collective-permute-start | bytes 798728 | tf_op jit(solution)/shard_map/ppermute | solution.py:189
  17.2 5.6 %collective-permute-done = bf16[1040,128]{1,0:T(8,128)(2,1)S(1)} collective-permute-done((bf16[1040,128]{1,0:T(8,128)(2,1)S(1)}, bf16[1040,128]{1,0:T(8,128)(2,1)S(1)}, u32[]{:S(2)}, u32[]{:S(2)}) %collective-permute-start) | collective-permute-done | bytes 266272 | tf_op jit(solution)/shard_map/ppermute | solution.py:189
  22.8 0.1 pad_maximum_fusion.2
  22.8 1.9 %collective-permute-start.1 = (bf16[2,1040,128]{2,1,0:T(8,128)(2,1)S(1)}, bf16[2,1040,128]{2,1,0:T(8,128)(2,1)S(1)}, u32[]{:S(2)}, u32[]{:S(2)}) collective-permute-start(bf16[2,1040,128]{2,1,0:T(8,128)(2,1)S(1)} %pad_maximum_fusion.2), channel_id=1, source_target_pairs={{0,4},{4,0},{8,12},{12,8},{16,20},{20,16},{24,28},{28,24},{32,36},... | collective-permute-start | bytes 1597448 | tf_op jit(solution)/shard_map/ppermute | solution.py:189
  24.7 1.9 %collective-permute-start.2 = (bf16[1040,128]{1,0:T(8,128)(2,1)S(1)}, bf16[1040,128]{1,0:T(8,128)(2,1)S(1)}, u32[]{:S(2)}, u32[]{:S(2)}) collective-permute-start(bf16[1040,128]{1,0:T(8,128)(2,1)S(1)} %get-tuple-element.32), channel_id=1, source_target_pairs={{0,8},{4,508},{8,16},{12,4},{16,24},{20,12},{24,32},{28,20},{32,40... | collective-permute-start | bytes 798728 | tf_op jit(solution)/shard_map/ppermute | solution.py:189
  26.7 0.0 copy-done.1
  26.7 0.2 fusion
  26.9 0.0 collective-permute-done.1
  27.0 16.7 %collective-permute-done.2 = bf16[1040,128]{1,0:T(8,128)(2,1)S(1)} collective-permute-done((bf16[1040,128]{1,0:T(8,128)(2,1)S(1)}, bf16[1040,128]{1,0:T(8,128)(2,1)S(1)}, u32[]{:S(2)}, u32[]{:S(2)}) %collective-permute-start.2) | collective-permute-done | bytes 266272 | tf_op jit(solution)/shard_map/ppermute | solution.py:189
  43.7 0.0 copy-start
  43.8 0.1 slice.46
  43.9 0.8 fusion.3
  44.6 4.7 %collective-permute-start.3 = (bf16[5,2,128,128]{3,2,1,0:T(8,128)(2,1)}, bf16[5,2,128,128]{3,2,1,0:T(8,128)(2,1)}, u32[]{:S(2)}, u32[]{:S(2)}) collective-permute-start(bf16[5,2,128,128]{3,2,1,0:T(8,128)(2,1)} %get-tuple-element.27), channel_id=1, source_target_pairs={{0,1},{1,2},{2,3},{3,0},{4,5},{5,6},{6,7},{7,4},{8,9},{9,10},{10,1... | collective-permute-start | bytes 983048 | tf_op jit(solution)/shard_map/ppermute | solution.py:24
  49.3 1.9 %collective-permute-start.4 = (bf16[5,2,128,128]{3,2,1,0:T(8,128)(2,1)S(1)}, bf16[5,2,128,128]{3,2,1,0:T(8,128)(2,1)}, u32[]{:S(2)}, u32[]{:S(2)}) collective-permute-start(bf16[5,2,128,128]{3,2,1,0:T(8,128)(2,1)S(1)} %get-tuple-element.28), channel_id=1, source_target_pairs={{0,3},{1,0},{2,1},{3,2},{4,7},{5,4},{6,5},{7,6},{8,11},{9,8},{10,9... | collective-permute-start | bytes 983048 | tf_op jit(solution)/shard_map/ppermute | solution.py:24
  51.2 0.0 copy-done
  51.3 0.7 fusion.4
  52.0 3.9 %collective-permute-start.5 = (f32[2,128,128]{2,1,0:T(8,128)}, f32[2,128,128]{2,1,0:T(8,128)}, u32[]{:S(2)}, u32[]{:S(2)}) collective-permute-start(f32[2,128,128]{2,1,0:T(8,128)} %get-tuple-element.29), channel_id=1, source_target_pairs={{0,1},{1,2},{2,3},{3,0},{4,5},{5,6},{6,7},{7,4},{8,9},{9,10},{10,1... | collective-permute-start | bytes 393224 | tf_op jit(solution)/shard_map/ppermute | solution.py:24
  55.9 3.3 %collective-permute-start.6 = (f32[2,128,128]{2,1,0:T(8,128)}, f32[2,128,128]{2,1,0:T(8,128)}, u32[]{:S(2)}, u32[]{:S(2)}) collective-permute-start(f32[2,128,128]{2,1,0:T(8,128)} %get-tuple-element.30), channel_id=1, source_target_pairs={{0,3},{1,0},{2,1},{3,2},{4,7},{5,4},{6,5},{7,6},{8,11},{9,8},{10,9... | collective-permute-start | bytes 393224 | tf_op jit(solution)/shard_map/ppermute | solution.py:24
  59.2 0.1 pad_maximum_fusion.4.weight_ref
  59.3 7.2 %collective-permute-done.5 = f32[2,128,128]{2,1,0:T(8,128)} collective-permute-done((f32[2,128,128]{2,1,0:T(8,128)}, f32[2,128,128]{2,1,0:T(8,128)}, u32[]{:S(2)}, u32[]{:S(2)}) %collective-permute-start.5) | collective-permute-done | bytes 131104 | tf_op jit(solution)/shard_map/ppermute | solution.py:24
  66.5 1.2 %collective-permute-done.6 = f32[2,128,128]{2,1,0:T(8,128)} collective-permute-done((f32[2,128,128]{2,1,0:T(8,128)}, f32[2,128,128]{2,1,0:T(8,128)}, u32[]{:S(2)}, u32[]{:S(2)}) %collective-permute-start.6) | collective-permute-done | bytes 131104 | tf_op jit(solution)/shard_map/ppermute | solution.py:24
  67.6 1.0 %pad_maximum_fusion.1.eps_ref = f32[12,128,128]{2,1,0:T(8,128)S(1)} fusion(f32[2,128,128]{2,1,0:T(8,128)} %collective-permute-done.6, f32[8,128,128]{2,1,0:T(8,128)S(1)} %copy-done, f32[2,128,128]{2,1,0:T(8,128)} %collective-permute-done.5), kind=kLoop, calls=%fused_computation.1 | loop fusion | flops 393216 | bytes 1572864 | tf_op jit(solution)/shard_map/concatenate | solution.py:33
  68.7 8.7 %shard_map.46 = (f32[4,128,128]{2,1,0:T(8,128)S(1)}, f32[4,1,128]{2,1,0:T(1,128)S(1)}, f32[4,4,128,128]{3,2,1,0:T(8,128)S(1)}, f32[4,2,128,128]{3,2,1,0:T(8,128)S(1)}, f32[4,2,128,128]{3,2,1,0:T(8,128)S(1)}) custom-call(f32[3]{0:T(128)S(1)} %pad_maximum_fusion.4.weight_ref, bf16[5,1040,128]{2,1,0:T(8,128)(2,1)S(1)} %slice_dynamic-update-slice_fusion.psi_ref, ...), custom_call_target="tpu_custom_call" | custom-call | flops 39321600 | bytes 2117632 | tf_op jit(solution)/shard_map/pallas_call | solution.py:172
  77.4 0.0 collective-permute-done.3
  77.4 0.0 collective-permute-done.4
  77.4 1.3 %pad_maximum_fusion.psi_ref = bf16[5,12,128,128]{3,2,1,0:T(8,128)(2,1)S(1)} fusion(bf16[5,2,128,128]{3,2,1,0:T(8,128)(2,1)} %collective-permute-done.4, bf16[5,8,128,128]{3,2,1,0:T(8,128)(2,1)S(1)} %bitcast.21, bf16[5,2,128,128]{3,2,1,0:T(8,128)(2,1)} %collective-permute-done.3), kind=kLoop, calls=%fused_computation | loop fusion | flops 1966080 | bytes 3932160 | tf_op jit(solution)/shard_map/concatenate | solution.py:33
  78.7 7.9 %shard_map.47 = f32[8,128,128]{2,1,0:T(8,128)} custom-call(f32[4,1,128]{2,1,0:T(1,128)S(1)} %get-tuple-element.22.weight_ref, bf16[5,12,128,128]{3,2,1,0:T(8,128)(2,1)S(1)} %pad_maximum_fusion.psi_ref, f32[12,128,128]{2,1,0:T(8,128)S(1)} %pad_maximum_fusion.1.eps_ref, f32[4,128,128]{2,1,0:T(8,128)S(1)} %get-tuple-element.23.refs_0_, ...), custom_call_target="tpu_custom_call" | custom-call | flops 58982400 | bytes 3276800 | tf_op jit(solution)/shard_map/pallas_call | solution.py:172
  (5 shorter events, 0.2 us)
Async XLA Ops:
  0.0 26.7 %copy-start.1 = (bf16[1,8,128,128]{3,2,1,0:T(8,128)(2,1)S(1)}, bf16[1,8,128,128]{3,2,1,0:T(8,128)(2,1)}, u32[]{:S(2)}) copy-start(bf16[1,8,128,128]{3,2,1,0:T(8,128)(2,1)} %param.6) | copy-start | bytes 786436
  2.6 20.2 %collective-permute-start = (bf16[1040,128]{1,0:T(8,128)(2,1)S(1)}, bf16[1040,128]{1,0:T(8,128)(2,1)S(1)}, u32[]{:S(2)}, u32[]{:S(2)}) collective-permute-start(bf16[1040,128]{1,0:T(8,128)(2,1)S(1)} %get-tuple-element.32), channel_id=1, source_target_pairs={{0,508},{4,8},{8,4},{12,16},{16,12},{20,24},{24,20},{28,32},{32,28... | collective-permute-start | bytes 798728 | tf_op jit(solution)/shard_map/ppermute | solution.py:189
  22.8 4.1 %collective-permute-start.1 = (bf16[2,1040,128]{2,1,0:T(8,128)(2,1)S(1)}, bf16[2,1040,128]{2,1,0:T(8,128)(2,1)S(1)}, u32[]{:S(2)}, u32[]{:S(2)}) collective-permute-start(bf16[2,1040,128]{2,1,0:T(8,128)(2,1)S(1)} %pad_maximum_fusion.2), channel_id=1, source_target_pairs={{0,4},{4,0},{8,12},{12,8},{16,20},{20,16},{24,28},{28,24},{32,36},... | collective-permute-start | bytes 1597448 | tf_op jit(solution)/shard_map/ppermute | solution.py:189
  24.7 18.9 %collective-permute-start.2 = (bf16[1040,128]{1,0:T(8,128)(2,1)S(1)}, bf16[1040,128]{1,0:T(8,128)(2,1)S(1)}, u32[]{:S(2)}, u32[]{:S(2)}) collective-permute-start(bf16[1040,128]{1,0:T(8,128)(2,1)S(1)} %get-tuple-element.32), channel_id=1, source_target_pairs={{0,8},{4,508},{8,16},{12,4},{16,24},{20,12},{24,32},{28,20},{32,40... | collective-permute-start | bytes 798728 | tf_op jit(solution)/shard_map/ppermute | solution.py:189
  43.7 7.5 %copy-start = (f32[8,128,128]{2,1,0:T(8,128)S(1)}, f32[8,128,128]{2,1,0:T(8,128)}, u32[]{:S(2)}) copy-start(f32[8,128,128]{2,1,0:T(8,128)} %eps_ref.1) | copy-start | bytes 1572868
  44.6 32.8 %collective-permute-start.3 = (bf16[5,2,128,128]{3,2,1,0:T(8,128)(2,1)}, bf16[5,2,128,128]{3,2,1,0:T(8,128)(2,1)}, u32[]{:S(2)}, u32[]{:S(2)}) collective-permute-start(bf16[5,2,128,128]{3,2,1,0:T(8,128)(2,1)} %get-tuple-element.27), channel_id=1, source_target_pairs={{0,1},{1,2},{2,3},{3,0},{4,5},{5,6},{6,7},{7,4},{8,9},{9,10},{10,1... | collective-permute-start | bytes 983048 | tf_op jit(solution)/shard_map/ppermute | solution.py:24
  49.3 28.1 %collective-permute-start.4 = (bf16[5,2,128,128]{3,2,1,0:T(8,128)(2,1)S(1)}, bf16[5,2,128,128]{3,2,1,0:T(8,128)(2,1)}, u32[]{:S(2)}, u32[]{:S(2)}) collective-permute-start(bf16[5,2,128,128]{3,2,1,0:T(8,128)(2,1)S(1)} %get-tuple-element.28), channel_id=1, source_target_pairs={{0,3},{1,0},{2,1},{3,2},{4,7},{5,4},{6,5},{7,6},{8,11},{9,8},{10,9... | collective-permute-start | bytes 983048 | tf_op jit(solution)/shard_map/ppermute | solution.py:24
  52.0 14.5 %collective-permute-start.5 = (f32[2,128,128]{2,1,0:T(8,128)}, f32[2,128,128]{2,1,0:T(8,128)}, u32[]{:S(2)}, u32[]{:S(2)}) collective-permute-start(f32[2,128,128]{2,1,0:T(8,128)} %get-tuple-element.29), channel_id=1, source_target_pairs={{0,1},{1,2},{2,3},{3,0},{4,5},{5,6},{6,7},{7,4},{8,9},{9,10},{10,1... | collective-permute-start | bytes 393224 | tf_op jit(solution)/shard_map/ppermute | solution.py:24
  55.9 11.7 %collective-permute-start.6 = (f32[2,128,128]{2,1,0:T(8,128)}, f32[2,128,128]{2,1,0:T(8,128)}, u32[]{:S(2)}, u32[]{:S(2)}) collective-permute-start(f32[2,128,128]{2,1,0:T(8,128)} %get-tuple-element.30), channel_id=1, source_target_pairs={{0,3},{1,0},{2,1},{3,2},{4,7},{5,4},{6,5},{7,6},{8,11},{9,8},{10,9... | collective-permute-start | bytes 393224 | tf_op jit(solution)/shard_map/ppermute | solution.py:24
where the time goes:
time: 87 us; the launch traced here: 86.7 us
  starting transfers between devices  32.2 us (37%)
  waiting for transfers between devices  30.7 us (35%)
  Pallas kernels  16.6 us (19%)
  other arithmetic  4.57 us (5%)
  local copies, waits for them, and re-layouts  1.75 us (2%)
    ppermute x3, waiting for transfers between devices, exchanged(): return lax.ppermute(x, axis, [(i, pairs_of(i) % size) for i in range(size)])  22.3 us
    ppermute x3, starting transfers between devices, exchanged(): return lax.ppermute(x, axis, [(i, pairs_of(i) % size) for i in range(size)])  18.4 us
    pallas_call x2, Pallas kernels, solve(): pl.pallas_call(functools.partial(solve_kernel, tuple(windows), sources),...  16.6 us
    ppermute x4, starting transfers between devices, shifted(): return lax.ppermute(x, axis, [(i, (i + by) % size) for i in range(size)])  13.8 us
    ppermute x4, waiting for transfers between devices, shifted(): return lax.ppermute(x, axis, [(i, (i + by) % size) for i in range(size)])  8.37 us
    concatenate x2, other arithmetic, z_halo(): return jnp.concatenate([before, x, after], axis=dim)  2.33 us
  transfers between devices with their start and end apart: 7, of which 4 were waited for; matrix products, arithmetic and copies ran while one was open for 2% of the time, Pallas kernels for 10%

commit v1 on v0

--- a/solution.py
+++ b/solution.py
@@ -92,7 +92,7 @@
             face_z[e] = (cur + eps_ref[start + e + 1]) * 0.5
             return carry
 
-        lax.fori_loop(0, size - 1, faces, 0)
+        lax.fori_loop(0, size - 1, faces, 0, unroll=True)
 
         for k in range(pairs):
             weight = weight_of[k]
@@ -103,7 +103,7 @@
                 first[e] = value / CHEB_CENTER
                 return carry
 
-            lax.fori_loop(dens_span[0], dens_span[1], density, 0)
+            lax.fori_loop(dens_span[0], dens_span[1], density, 0, unroll=True)
 
             def sweep_one(e, carry):
                 center = first[e]
@@ -116,7 +116,7 @@
 
             lo, hi = sweep_span
             flux[...] = face_z[lo - 1] * (first[lo] - first[lo - 1])
-            lax.fori_loop(lo, hi, sweep_one, 0)
+            lax.fori_loop(lo, hi, sweep_one, 0, unroll=2)
             if sources is not None:
                 for j, e in enumerate((1, 2, size - 3, size - 2)):
                     kept_second[k, j] = second[e]
@@ -139,7 +139,7 @@
                 return carry
 
             flux[...] = face_z[1] * (second[2] - second[1])
-            lax.fori_loop(HALO, size - HALO, sweep_two, 0)
+            lax.fori_loop(HALO, size - HALO, sweep_two, 0, unroll=2)
         out_ref[pl.ds(at, count)] = -out_ref[pl.ds(at, count)]
     if middle_ref is not None:
         out_ref[pl.ds(HALO, middle_ref.shape[0])] = middle_ref[...]

time: 87 us -> 79.8 us (0.917)
  Pallas kernels: 16.6 us -> 9.42 us
    pallas_call x2, Pallas kernels: 16.6 us -> 9.42 us  [solve(): pl.pallas_call(functools.partial(solve_kernel, tuple(windows), sources),...]
  transfers between devices with their start and end apart: 7 -> 7, of which waited for: 4 -> 4; matrix products, arithmetic and copies ran while one was open for 2% -> 3% of each run, Pallas kernels for 10% -> 6%
where the time goes in v1:
time: 79.8 us; the launch traced here: 79.4 us
  starting transfers between devices  32.2 us (40%)
  waiting for transfers between devices  30.7 us (38%)
  Pallas kernels  9.42 us (12%)
  other arithmetic  4.57 us (6%)
  local copies, waits for them, and re-layouts  1.75 us (2%)
  between operations  0.85 us (1%)
    ppermute x3, waiting for transfers between devices, exchanged(): return lax.ppermute(x, axis, [(i, pairs_of(i) % size) for i in range(size)])  22.3 us
    ppermute x3, starting transfers between devices, exchanged(): return lax.ppermute(x, axis, [(i, pairs_of(i) % size) for i in range(size)])  18.4 us
    ppermute x4, starting transfers between devices, shifted(): return lax.ppermute(x, axis, [(i, (i + by) % size) for i in range(size)])  13.8 us
    pallas_call x2, Pallas kernels, solve(): pl.pallas_call(functools.partial(solve_kernel, tuple(windows), sources),...  9.42 us
    ppermute x4, waiting for transfers between devices, shifted(): return lax.ppermute(x, axis, [(i, (i + by) % size) for i in range(size)])  8.37 us
    concatenate x2, other arithmetic, z_halo(): return jnp.concatenate([before, x, after], axis=dim)  2.33 us
  transfers between devices with their start and end apart: 7, of which 4 were waited for; matrix products, arithmetic and copies ran while one was open for 3% of the time, Pallas kernels for 6%

profile of v1, /device:TPU:64, one launch (start us, length us, event | category | flops | bytes accessed | tf_op | source)
XLA Modules:
  0.0 79.4 jit_solution(1214470275504985982)
XLA Ops:
  0.0 0.0 copy-start.1
  0.0 0.7 convert_bitcast_fusion
  1.4 1.0 %broadcast_multiply_fusion = bf16[1024,128]{1,0:T(8,128)(2,1)S(1)} fusion(bf16[]{:T(256)} %bitcast.5, bf16[1,8,128,128]{3,2,1,0:T(8,128)(2,1)} %param.6), kind=kLoop, calls=%fused_computation.9 | loop fusion | flops 131072 | bytes 524290 | tf_op jit(solution)/shard_map/mul | solution.py:203
  2.4 0.2 fusion.2
  2.6 14.6 %collective-permute-start = (bf16[1040,128]{1,0:T(8,128)(2,1)S(1)}, bf16[1040,128]{1,0:T(8,128)(2,1)S(1)}, u32[]{:S(2)}, u32[]{:S(2)}) collective-permute-start(bf16[1040,128]{1,0:T(8,128)(2,1)S(1)} %get-tuple-element.32), channel_id=1, source_target_pairs={{0,508},{4,8},{8,4},{12,16},{16,12},{20,24},{24,20},{28,32},{32,28... | collective-permute-start | bytes 798728 | tf_op jit(solution)/shard_map/ppermute | solution.py:189
  17.2 5.6 %collective-permute-done = bf16[1040,128]{1,0:T(8,128)(2,1)S(1)} collective-permute-done((bf16[1040,128]{1,0:T(8,128)(2,1)S(1)}, bf16[1040,128]{1,0:T(8,128)(2,1)S(1)}, u32[]{:S(2)}, u32[]{:S(2)}) %collective-permute-start) | collective-permute-done | bytes 266272 | tf_op jit(solution)/shard_map/ppermute | solution.py:189
  22.8 0.1 pad_maximum_fusion.2
  22.8 1.9 %collective-permute-start.1 = (bf16[2,1040,128]{2,1,0:T(8,128)(2,1)S(1)}, bf16[2,1040,128]{2,1,0:T(8,128)(2,1)S(1)}, u32[]{:S(2)}, u32[]{:S(2)}) collective-permute-start(bf16[2,1040,128]{2,1,0:T(8,128)(2,1)S(1)} %pad_maximum_fusion.2), channel_id=1, source_target_pairs={{0,4},{4,0},{8,12},{12,8},{16,20},{20,16},{24,28},{28,24},{32,36},... | collective-permute-start | bytes 1597448 | tf_op jit(solution)/shard_map/ppermute | solution.py:189
  24.7 1.9 %collective-permute-start.2 = (bf16[1040,128]{1,0:T(8,128)(2,1)S(1)}, bf16[1040,128]{1,0:T(8,128)(2,1)S(1)}, u32[]{:S(2)}, u32[]{:S(2)}) collective-permute-start(bf16[1040,128]{1,0:T(8,128)(2,1)S(1)} %get-tuple-element.32), channel_id=1, source_target_pairs={{0,8},{4,508},{8,16},{12,4},{16,24},{20,12},{24,32},{28,20},{32,40... | collective-permute-start | bytes 798728 | tf_op jit(solution)/shard_map/ppermute | solution.py:189
  26.7 0.0 copy-done.1
  26.7 0.2 fusion
  26.9 0.0 collective-permute-done.1
  27.0 16.7 %collective-permute-done.2 = bf16[1040,128]{1,0:T(8,128)(2,1)S(1)} collective-permute-done((bf16[1040,128]{1,0:T(8,128)(2,1)S(1)}, bf16[1040,128]{1,0:T(8,128)(2,1)S(1)}, u32[]{:S(2)}, u32[]{:S(2)}) %collective-permute-start.2) | collective-permute-done | bytes 266272 | tf_op jit(solution)/shard_map/ppermute | solution.py:189
  43.7 0.0 copy-start
  43.8 0.1 slice.46
  43.9 0.8 fusion.3
  44.6 4.7 %collective-permute-start.3 = (bf16[5,2,128,128]{3,2,1,0:T(8,128)(2,1)}, bf16[5,2,128,128]{3,2,1,0:T(8,128)(2,1)}, u32[]{:S(2)}, u32[]{:S(2)}) collective-permute-start(bf16[5,2,128,128]{3,2,1,0:T(8,128)(2,1)} %get-tuple-element.27), channel_id=1, source_target_pairs={{0,1},{1,2},{2,3},{3,0},{4,5},{5,6},{6,7},{7,4},{8,9},{9,10},{10,1... | collective-permute-start | bytes 983048 | tf_op jit(solution)/shard_map/ppermute | solution.py:24
  49.3 1.9 %collective-permute-start.4 = (bf16[5,2,128,128]{3,2,1,0:T(8,128)(2,1)S(1)}, bf16[5,2,128,128]{3,2,1,0:T(8,128)(2,1)}, u32[]{:S(2)}, u32[]{:S(2)}) collective-permute-start(bf16[5,2,128,128]{3,2,1,0:T(8,128)(2,1)S(1)} %get-tuple-element.28), channel_id=1, source_target_pairs={{0,3},{1,0},{2,1},{3,2},{4,7},{5,4},{6,5},{7,6},{8,11},{9,8},{10,9... | collective-permute-start | bytes 983048 | tf_op jit(solution)/shard_map/ppermute | solution.py:24
  51.2 0.0 copy-done
  51.3 0.7 fusion.4
  52.0 3.9 %collective-permute-start.5 = (f32[2,128,128]{2,1,0:T(8,128)}, f32[2,128,128]{2,1,0:T(8,128)}, u32[]{:S(2)}, u32[]{:S(2)}) collective-permute-start(f32[2,128,128]{2,1,0:T(8,128)} %get-tuple-element.29), channel_id=1, source_target_pairs={{0,1},{1,2},{2,3},{3,0},{4,5},{5,6},{6,7},{7,4},{8,9},{9,10},{10,1... | collective-permute-start | bytes 393224 | tf_op jit(solution)/shard_map/ppermute | solution.py:24
  55.9 3.3 %collective-permute-start.6 = (f32[2,128,128]{2,1,0:T(8,128)}, f32[2,128,128]{2,1,0:T(8,128)}, u32[]{:S(2)}, u32[]{:S(2)}) collective-permute-start(f32[2,128,128]{2,1,0:T(8,128)} %get-tuple-element.30), channel_id=1, source_target_pairs={{0,3},{1,0},{2,1},{3,2},{4,7},{5,4},{6,5},{7,6},{8,11},{9,8},{10,9... | collective-permute-start | bytes 393224 | tf_op jit(solution)/shard_map/ppermute | solution.py:24
  59.2 0.1 pad_maximum_fusion.4.weight_ref
  59.3 7.2 %collective-permute-done.5 = f32[2,128,128]{2,1,0:T(8,128)} collective-permute-done((f32[2,128,128]{2,1,0:T(8,128)}, f32[2,128,128]{2,1,0:T(8,128)}, u32[]{:S(2)}, u32[]{:S(2)}) %collective-permute-start.5) | collective-permute-done | bytes 131104 | tf_op jit(solution)/shard_map/ppermute | solution.py:24
  66.5 1.2 %collective-permute-done.6 = f32[2,128,128]{2,1,0:T(8,128)} collective-permute-done((f32[2,128,128]{2,1,0:T(8,128)}, f32[2,128,128]{2,1,0:T(8,128)}, u32[]{:S(2)}, u32[]{:S(2)}) %collective-permute-start.6) | collective-permute-done | bytes 131104 | tf_op jit(solution)/shard_map/ppermute | solution.py:24
  67.6 1.0 %pad_maximum_fusion.1.eps_ref = f32[12,128,128]{2,1,0:T(8,128)S(1)} fusion(f32[2,128,128]{2,1,0:T(8,128)} %collective-permute-done.6, f32[8,128,128]{2,1,0:T(8,128)S(1)} %copy-done, f32[2,128,128]{2,1,0:T(8,128)} %collective-permute-done.5), kind=kLoop, calls=%fused_computation.1 | loop fusion | flops 393216 | bytes 1572864 | tf_op jit(solution)/shard_map/concatenate | solution.py:33
  68.7 5.1 %shard_map.46 = (f32[4,128,128]{2,1,0:T(8,128)S(1)}, f32[4,1,128]{2,1,0:T(1,128)S(1)}, f32[4,4,128,128]{3,2,1,0:T(8,128)S(1)}, f32[4,2,128,128]{3,2,1,0:T(8,128)S(1)}, f32[4,2,128,128]{3,2,1,0:T(8,128)S(1)}) custom-call(f32[3]{0:T(128)S(1)} %pad_maximum_fusion.4.weight_ref, bf16[5,1040,128]{2,1,0:T(8,128)(2,1)S(1)} %slice_dynamic-update-slice_fusion.psi_ref, ...), custom_call_target="tpu_custom_call" | custom-call | flops 39321600 | bytes 2117632 | tf_op jit(solution)/shard_map/pallas_call | solution.py:172
  73.8 0.0 collective-permute-done.3
  73.8 0.0 collective-permute-done.4
  73.8 1.3 %pad_maximum_fusion.psi_ref = bf16[5,12,128,128]{3,2,1,0:T(8,128)(2,1)S(1)} fusion(bf16[5,2,128,128]{3,2,1,0:T(8,128)(2,1)} %collective-permute-done.4, bf16[5,8,128,128]{3,2,1,0:T(8,128)(2,1)S(1)} %bitcast.21, bf16[5,2,128,128]{3,2,1,0:T(8,128)(2,1)} %collective-permute-done.3), kind=kLoop, calls=%fused_computation | loop fusion | flops 1966080 | bytes 3932160 | tf_op jit(solution)/shard_map/concatenate | solution.py:33
  75.1 4.3 %shard_map.47 = f32[8,128,128]{2,1,0:T(8,128)} custom-call(f32[4,1,128]{2,1,0:T(1,128)S(1)} %get-tuple-element.22.weight_ref, bf16[5,12,128,128]{3,2,1,0:T(8,128)(2,1)S(1)} %pad_maximum_fusion.psi_ref, f32[12,128,128]{2,1,0:T(8,128)S(1)} %pad_maximum_fusion.1.eps_ref, f32[4,128,128]{2,1,0:T(8,128)S(1)} %get-tuple-element.23.refs_0_, ...), custom_call_target="tpu_custom_call" | custom-call | flops 58982400 | bytes 3276800 | tf_op jit(solution)/shard_map/pallas_call | solution.py:172
  (5 shorter events, 0.2 us)
Async XLA Ops:
  0.0 26.7 %copy-start.1 = (bf16[1,8,128,128]{3,2,1,0:T(8,128)(2,1)S(1)}, bf16[1,8,128,128]{3,2,1,0:T(8,128)(2,1)}, u32[]{:S(2)}) copy-start(bf16[1,8,128,128]{3,2,1,0:T(8,128)(2,1)} %param.6) | copy-start | bytes 786436
  2.6 20.2 %collective-permute-start = (bf16[1040,128]{1,0:T(8,128)(2,1)S(1)}, bf16[1040,128]{1,0:T(8,128)(2,1)S(1)}, u32[]{:S(2)}, u32[]{:S(2)}) collective-permute-start(bf16[1040,128]{1,0:T(8,128)(2,1)S(1)} %get-tuple-element.32), channel_id=1, source_target_pairs={{0,508},{4,8},{8,4},{12,16},{16,12},{20,24},{24,20},{28,32},{32,28... | collective-permute-start | bytes 798728 | tf_op jit(solution)/shard_map/ppermute | solution.py:189
  22.8 4.1 %collective-permute-start.1 = (bf16[2,1040,128]{2,1,0:T(8,128)(2,1)S(1)}, bf16[2,1040,128]{2,1,0:T(8,128)(2,1)S(1)}, u32[]{:S(2)}, u32[]{:S(2)}) collective-permute-start(bf16[2,1040,128]{2,1,0:T(8,128)(2,1)S(1)} %pad_maximum_fusion.2), channel_id=1, source_target_pairs={{0,4},{4,0},{8,12},{12,8},{16,20},{20,16},{24,28},{28,24},{32,36},... | collective-permute-start | bytes 1597448 | tf_op jit(solution)/shard_map/ppermute | solution.py:189
  24.7 18.9 %collective-permute-start.2 = (bf16[1040,128]{1,0:T(8,128)(2,1)S(1)}, bf16[1040,128]{1,0:T(8,128)(2,1)S(1)}, u32[]{:S(2)}, u32[]{:S(2)}) collective-permute-start(bf16[1040,128]{1,0:T(8,128)(2,1)S(1)} %get-tuple-element.32), channel_id=1, source_target_pairs={{0,8},{4,508},{8,16},{12,4},{16,24},{20,12},{24,32},{28,20},{32,40... | collective-permute-start | bytes 798728 | tf_op jit(solution)/shard_map/ppermute | solution.py:189
  43.7 7.5 %copy-start = (f32[8,128,128]{2,1,0:T(8,128)S(1)}, f32[8,128,128]{2,1,0:T(8,128)}, u32[]{:S(2)}) copy-start(f32[8,128,128]{2,1,0:T(8,128)} %eps_ref.1) | copy-start | bytes 1572868
  44.6 29.2 %collective-permute-start.3 = (bf16[5,2,128,128]{3,2,1,0:T(8,128)(2,1)}, bf16[5,2,128,128]{3,2,1,0:T(8,128)(2,1)}, u32[]{:S(2)}, u32[]{:S(2)}) collective-permute-start(bf16[5,2,128,128]{3,2,1,0:T(8,128)(2,1)} %get-tuple-element.27), channel_id=1, source_target_pairs={{0,1},{1,2},{2,3},{3,0},{4,5},{5,6},{6,7},{7,4},{8,9},{9,10},{10,1... | collective-permute-start | bytes 983048 | tf_op jit(solution)/shard_map/ppermute | solution.py:24
  49.3 24.5 %collective-permute-start.4 = (bf16[5,2,128,128]{3,2,1,0:T(8,128)(2,1)S(1)}, bf16[5,2,128,128]{3,2,1,0:T(8,128)(2,1)}, u32[]{:S(2)}, u32[]{:S(2)}) collective-permute-start(bf16[5,2,128,128]{3,2,1,0:T(8,128)(2,1)S(1)} %get-tuple-element.28), channel_id=1, source_target_pairs={{0,3},{1,0},{2,1},{3,2},{4,7},{5,4},{6,5},{7,6},{8,11},{9,8},{10,9... | collective-permute-start | bytes 983048 | tf_op jit(solution)/shard_map/ppermute | solution.py:24
  52.0 14.5 %collective-permute-start.5 = (f32[2,128,128]{2,1,0:T(8,128)}, f32[2,128,128]{2,1,0:T(8,128)}, u32[]{:S(2)}, u32[]{:S(2)}) collective-permute-start(f32[2,128,128]{2,1,0:T(8,128)} %get-tuple-element.29), channel_id=1, source_target_pairs={{0,1},{1,2},{2,3},{3,0},{4,5},{5,6},{6,7},{7,4},{8,9},{9,10},{10,1... | collective-permute-start | bytes 393224 | tf_op jit(solution)/shard_map/ppermute | solution.py:24
  55.9 11.7 %collective-permute-start.6 = (f32[2,128,128]{2,1,0:T(8,128)}, f32[2,128,128]{2,1,0:T(8,128)}, u32[]{:S(2)}, u32[]{:S(2)}) collective-permute-start(f32[2,128,128]{2,1,0:T(8,128)} %get-tuple-element.30), channel_id=1, source_target_pairs={{0,3},{1,0},{2,1},{3,2},{4,7},{5,4},{6,5},{7,6},{8,11},{9,8},{10,9... | collective-permute-start | bytes 393224 | tf_op jit(solution)/shard_map/ppermute | solution.py:24

commit v2 on v1

--- a/solution.py
+++ b/solution.py
@@ -103,7 +103,7 @@
                 first[e] = value / CHEB_CENTER
                 return carry
 
-            lax.fori_loop(dens_span[0], dens_span[1], density, 0, unroll=True)
+            lax.fori_loop(dens_span[0], dens_span[1], density, 0, unroll=2)
 
             def sweep_one(e, carry):
                 center = first[e]
@@ -116,7 +116,7 @@
 
             lo, hi = sweep_span
             flux[...] = face_z[lo - 1] * (first[lo] - first[lo - 1])
-            lax.fori_loop(lo, hi, sweep_one, 0, unroll=2)
+            lax.fori_loop(lo, hi, sweep_one, 0, unroll=True)
             if sources is not None:
                 for j, e in enumerate((1, 2, size - 3, size - 2)):
                     kept_second[k, j] = second[e]
@@ -139,7 +139,7 @@
                 return carry
 
             flux[...] = face_z[1] * (second[2] - second[1])
-            lax.fori_loop(HALO, size - HALO, sweep_two, 0, unroll=2)
+            lax.fori_loop(HALO, size - HALO, sweep_two, 0, unroll=True)
         out_ref[pl.ds(at, count)] = -out_ref[pl.ds(at, count)]
     if middle_ref is not None:
         out_ref[pl.ds(HALO, middle_ref.shape[0])] = middle_ref[...]

time: 79.8 us -> 79.2 us (level)
  no operation moved by 1% of the time
where the time goes in v2:
time: 79.2 us; the launch traced here: 78.9 us
  starting transfers between devices  32.2 us (41%)
  waiting for transfers between devices  30.7 us (39%)
  Pallas kernels  8.87 us (11%)
  other arithmetic  4.57 us (6%)
  local copies, waits for them, and re-layouts  1.75 us (2%)
  between operations  0.84 us (1%)
    ppermute x3, waiting for transfers between devices, exchanged(): return lax.ppermute(x, axis, [(i, pairs_of(i) % size) for i in range(size)])  22.3 us
    ppermute x3, starting transfers between devices, exchanged(): return lax.ppermute(x, axis, [(i, pairs_of(i) % size) for i in range(size)])  18.4 us
    ppermute x4, starting transfers between devices, shifted(): return lax.ppermute(x, axis, [(i, (i + by) % size) for i in range(size)])  13.8 us
    pallas_call x2, Pallas kernels, solve(): pl.pallas_call(functools.partial(solve_kernel, tuple(windows), sources),...  8.87 us
    ppermute x4, waiting for transfers between devices, shifted(): return lax.ppermute(x, axis, [(i, (i + by) % size) for i in range(size)])  8.37 us
    concatenate x2, other arithmetic, z_halo(): return jnp.concatenate([before, x, after], axis=dim)  2.33 us
  transfers between devices with their start and end apart: 7, of which 4 were waited for; matrix products, arithmetic and copies ran while one was open for 3% of the time, Pallas kernels for 6%

profile of v2, /device:TPU:64, one launch (start us, length us, event | category | flops | bytes accessed | tf_op | source)
XLA Modules:
  0.0 78.9 jit_solution(2070508276817283242)
XLA Ops:
  0.0 0.0 copy-start.1
  0.0 0.7 convert_bitcast_fusion
  1.4 1.0 %broadcast_multiply_fusion = bf16[1024,128]{1,0:T(8,128)(2,1)S(1)} fusion(bf16[]{:T(256)} %bitcast.5, bf16[1,8,128,128]{3,2,1,0:T(8,128)(2,1)} %param.6), kind=kLoop, calls=%fused_computation.9 | loop fusion | flops 131072 | bytes 524290 | tf_op jit(solution)/shard_map/mul | solution.py:203
  2.4 0.2 fusion.2
  2.6 14.6 %collective-permute-start = (bf16[1040,128]{1,0:T(8,128)(2,1)S(1)}, bf16[1040,128]{1,0:T(8,128)(2,1)S(1)}, u32[]{:S(2)}, u32[]{:S(2)}) collective-permute-start(bf16[1040,128]{1,0:T(8,128)(2,1)S(1)} %get-tuple-element.32), channel_id=1, source_target_pairs={{0,508},{4,8},{8,4},{12,16},{16,12},{20,24},{24,20},{28,32},{32,28... | collective-permute-start | bytes 798728 | tf_op jit(solution)/shard_map/ppermute | solution.py:189
  17.2 5.6 %collective-permute-done = bf16[1040,128]{1,0:T(8,128)(2,1)S(1)} collective-permute-done((bf16[1040,128]{1,0:T(8,128)(2,1)S(1)}, bf16[1040,128]{1,0:T(8,128)(2,1)S(1)}, u32[]{:S(2)}, u32[]{:S(2)}) %collective-permute-start) | collective-permute-done | bytes 266272 | tf_op jit(solution)/shard_map/ppermute | solution.py:189
  22.8 0.1 pad_maximum_fusion.2
  22.8 1.9 %collective-permute-start.1 = (bf16[2,1040,128]{2,1,0:T(8,128)(2,1)S(1)}, bf16[2,1040,128]{2,1,0:T(8,128)(2,1)S(1)}, u32[]{:S(2)}, u32[]{:S(2)}) collective-permute-start(bf16[2,1040,128]{2,1,0:T(8,128)(2,1)S(1)} %pad_maximum_fusion.2), channel_id=1, source_target_pairs={{0,4},{4,0},{8,12},{12,8},{16,20},{20,16},{24,28},{28,24},{32,36},... | collective-permute-start | bytes 1597448 | tf_op jit(solution)/shard_map/ppermute | solution.py:189
  24.7 1.9 %collective-permute-start.2 = (bf16[1040,128]{1,0:T(8,128)(2,1)S(1)}, bf16[1040,128]{1,0:T(8,128)(2,1)S(1)}, u32[]{:S(2)}, u32[]{:S(2)}) collective-permute-start(bf16[1040,128]{1,0:T(8,128)(2,1)S(1)} %get-tuple-element.32), channel_id=1, source_target_pairs={{0,8},{4,508},{8,16},{12,4},{16,24},{20,12},{24,32},{28,20},{32,40... | collective-permute-start | bytes 798728 | tf_op jit(solution)/shard_map/ppermute | solution.py:189
  26.7 0.0 copy-done.1
  26.7 0.2 fusion
  26.9 0.0 collective-permute-done.1
  27.0 16.7 %collective-permute-done.2 = bf16[1040,128]{1,0:T(8,128)(2,1)S(1)} collective-permute-done((bf16[1040,128]{1,0:T(8,128)(2,1)S(1)}, bf16[1040,128]{1,0:T(8,128)(2,1)S(1)}, u32[]{:S(2)}, u32[]{:S(2)}) %collective-permute-start.2) | collective-permute-done | bytes 266272 | tf_op jit(solution)/shard_map/ppermute | solution.py:189
  43.7 0.0 copy-start
  43.8 0.1 slice.46
  43.9 0.8 fusion.3
  44.6 4.7 %collective-permute-start.3 = (bf16[5,2,128,128]{3,2,1,0:T(8,128)(2,1)}, bf16[5,2,128,128]{3,2,1,0:T(8,128)(2,1)}, u32[]{:S(2)}, u32[]{:S(2)}) collective-permute-start(bf16[5,2,128,128]{3,2,1,0:T(8,128)(2,1)} %get-tuple-element.27), channel_id=1, source_target_pairs={{0,1},{1,2},{2,3},{3,0},{4,5},{5,6},{6,7},{7,4},{8,9},{9,10},{10,1... | collective-permute-start | bytes 983048 | tf_op jit(solution)/shard_map/ppermute | solution.py:24
  49.3 1.9 %collective-permute-start.4 = (bf16[5,2,128,128]{3,2,1,0:T(8,128)(2,1)S(1)}, bf16[5,2,128,128]{3,2,1,0:T(8,128)(2,1)}, u32[]{:S(2)}, u32[]{:S(2)}) collective-permute-start(bf16[5,2,128,128]{3,2,1,0:T(8,128)(2,1)S(1)} %get-tuple-element.28), channel_id=1, source_target_pairs={{0,3},{1,0},{2,1},{3,2},{4,7},{5,4},{6,5},{7,6},{8,11},{9,8},{10,9... | collective-permute-start | bytes 983048 | tf_op jit(solution)/shard_map/ppermute | solution.py:24
  51.2 0.0 copy-done
  51.3 0.7 fusion.4
  52.0 3.9 %collective-permute-start.5 = (f32[2,128,128]{2,1,0:T(8,128)}, f32[2,128,128]{2,1,0:T(8,128)}, u32[]{:S(2)}, u32[]{:S(2)}) collective-permute-start(f32[2,128,128]{2,1,0:T(8,128)} %get-tuple-element.29), channel_id=1, source_target_pairs={{0,1},{1,2},{2,3},{3,0},{4,5},{5,6},{6,7},{7,4},{8,9},{9,10},{10,1... | collective-permute-start | bytes 393224 | tf_op jit(solution)/shard_map/ppermute | solution.py:24
  55.9 3.3 %collective-permute-start.6 = (f32[2,128,128]{2,1,0:T(8,128)}, f32[2,128,128]{2,1,0:T(8,128)}, u32[]{:S(2)}, u32[]{:S(2)}) collective-permute-start(f32[2,128,128]{2,1,0:T(8,128)} %get-tuple-element.30), channel_id=1, source_target_pairs={{0,3},{1,0},{2,1},{3,2},{4,7},{5,4},{6,5},{7,6},{8,11},{9,8},{10,9... | collective-permute-start | bytes 393224 | tf_op jit(solution)/shard_map/ppermute | solution.py:24
  59.2 0.1 pad_maximum_fusion.4.weight_ref
  59.3 7.2 %collective-permute-done.5 = f32[2,128,128]{2,1,0:T(8,128)} collective-permute-done((f32[2,128,128]{2,1,0:T(8,128)}, f32[2,128,128]{2,1,0:T(8,128)}, u32[]{:S(2)}, u32[]{:S(2)}) %collective-permute-start.5) | collective-permute-done | bytes 131104 | tf_op jit(solution)/shard_map/ppermute | solution.py:24
  66.5 1.2 %collective-permute-done.6 = f32[2,128,128]{2,1,0:T(8,128)} collective-permute-done((f32[2,128,128]{2,1,0:T(8,128)}, f32[2,128,128]{2,1,0:T(8,128)}, u32[]{:S(2)}, u32[]{:S(2)}) %collective-permute-start.6) | collective-permute-done | bytes 131104 | tf_op jit(solution)/shard_map/ppermute | solution.py:24
  67.6 1.0 %pad_maximum_fusion.1.eps_ref = f32[12,128,128]{2,1,0:T(8,128)S(1)} fusion(f32[2,128,128]{2,1,0:T(8,128)} %collective-permute-done.6, f32[8,128,128]{2,1,0:T(8,128)S(1)} %copy-done, f32[2,128,128]{2,1,0:T(8,128)} %collective-permute-done.5), kind=kLoop, calls=%fused_computation.1 | loop fusion | flops 393216 | bytes 1572864 | tf_op jit(solution)/shard_map/concatenate | solution.py:33
  68.7 4.6 %shard_map.46 = (f32[4,128,128]{2,1,0:T(8,128)S(1)}, f32[4,1,128]{2,1,0:T(1,128)S(1)}, f32[4,4,128,128]{3,2,1,0:T(8,128)S(1)}, f32[4,2,128,128]{3,2,1,0:T(8,128)S(1)}, f32[4,2,128,128]{3,2,1,0:T(8,128)S(1)}) custom-call(f32[3]{0:T(128)S(1)} %pad_maximum_fusion.4.weight_ref, bf16[5,1040,128]{2,1,0:T(8,128)(2,1)S(1)} %slice_dynamic-update-slice_fusion.psi_ref, ...), custom_call_target="tpu_custom_call" | custom-call | flops 39321600 | bytes 2117632 | tf_op jit(solution)/shard_map/pallas_call | solution.py:172
  73.3 0.0 collective-permute-done.3
  73.3 0.0 collective-permute-done.4
  73.3 1.3 %pad_maximum_fusion.psi_ref = bf16[5,12,128,128]{3,2,1,0:T(8,128)(2,1)S(1)} fusion(bf16[5,2,128,128]{3,2,1,0:T(8,128)(2,1)} %collective-permute-done.4, bf16[5,8,128,128]{3,2,1,0:T(8,128)(2,1)S(1)} %bitcast.21, bf16[5,2,128,128]{3,2,1,0:T(8,128)(2,1)} %collective-permute-done.3), kind=kLoop, calls=%fused_computation | loop fusion | flops 1966080 | bytes 3932160 | tf_op jit(solution)/shard_map/concatenate | solution.py:33
  74.7 4.2 %shard_map.47 = f32[8,128,128]{2,1,0:T(8,128)} custom-call(f32[4,1,128]{2,1,0:T(1,128)S(1)} %get-tuple-element.22.weight_ref, bf16[5,12,128,128]{3,2,1,0:T(8,128)(2,1)S(1)} %pad_maximum_fusion.psi_ref, f32[12,128,128]{2,1,0:T(8,128)S(1)} %pad_maximum_fusion.1.eps_ref, f32[4,128,128]{2,1,0:T(8,128)S(1)} %get-tuple-element.23.refs_0_, ...), custom_call_target="tpu_custom_call" | custom-call | flops 58982400 | bytes 3276800 | tf_op jit(solution)/shard_map/pallas_call | solution.py:172
  (5 shorter events, 0.2 us)
Async XLA Ops:
  0.0 26.7 %copy-start.1 = (bf16[1,8,128,128]{3,2,1,0:T(8,128)(2,1)S(1)}, bf16[1,8,128,128]{3,2,1,0:T(8,128)(2,1)}, u32[]{:S(2)}) copy-start(bf16[1,8,128,128]{3,2,1,0:T(8,128)(2,1)} %param.6) | copy-start | bytes 786436
  2.6 20.2 %collective-permute-start = (bf16[1040,128]{1,0:T(8,128)(2,1)S(1)}, bf16[1040,128]{1,0:T(8,128)(2,1)S(1)}, u32[]{:S(2)}, u32[]{:S(2)}) collective-permute-start(bf16[1040,128]{1,0:T(8,128)(2,1)S(1)} %get-tuple-element.32), channel_id=1, source_target_pairs={{0,508},{4,8},{8,4},{12,16},{16,12},{20,24},{24,20},{28,32},{32,28... | collective-permute-start | bytes 798728 | tf_op jit(solution)/shard_map/ppermute | solution.py:189
  22.8 4.1 %collective-permute-start.1 = (bf16[2,1040,128]{2,1,0:T(8,128)(2,1)S(1)}, bf16[2,1040,128]{2,1,0:T(8,128)(2,1)S(1)}, u32[]{:S(2)}, u32[]{:S(2)}) collective-permute-start(bf16[2,1040,128]{2,1,0:T(8,128)(2,1)S(1)} %pad_maximum_fusion.2), channel_id=1, source_target_pairs={{0,4},{4,0},{8,12},{12,8},{16,20},{20,16},{24,28},{28,24},{32,36},... | collective-permute-start | bytes 1597448 | tf_op jit(solution)/shard_map/ppermute | solution.py:189
  24.7 18.9 %collective-permute-start.2 = (bf16[1040,128]{1,0:T(8,128)(2,1)S(1)}, bf16[1040,128]{1,0:T(8,128)(2,1)S(1)}, u32[]{:S(2)}, u32[]{:S(2)}) collective-permute-start(bf16[1040,128]{1,0:T(8,128)(2,1)S(1)} %get-tuple-element.32), channel_id=1, source_target_pairs={{0,8},{4,508},{8,16},{12,4},{16,24},{20,12},{24,32},{28,20},{32,40... | collective-permute-start | bytes 798728 | tf_op jit(solution)/shard_map/ppermute | solution.py:189
  43.7 7.5 %copy-start = (f32[8,128,128]{2,1,0:T(8,128)S(1)}, f32[8,128,128]{2,1,0:T(8,128)}, u32[]{:S(2)}) copy-start(f32[8,128,128]{2,1,0:T(8,128)} %eps_ref.1) | copy-start | bytes 1572868
  44.6 28.7 %collective-permute-start.3 = (bf16[5,2,128,128]{3,2,1,0:T(8,128)(2,1)}, bf16[5,2,128,128]{3,2,1,0:T(8,128)(2,1)}, u32[]{:S(2)}, u32[]{:S(2)}) collective-permute-start(bf16[5,2,128,128]{3,2,1,0:T(8,128)(2,1)} %get-tuple-element.27), channel_id=1, source_target_pairs={{0,1},{1,2},{2,3},{3,0},{4,5},{5,6},{6,7},{7,4},{8,9},{9,10},{10,1... | collective-permute-start | bytes 983048 | tf_op jit(solution)/shard_map/ppermute | solution.py:24
  49.3 24.0 %collective-permute-start.4 = (bf16[5,2,128,128]{3,2,1,0:T(8,128)(2,1)S(1)}, bf16[5,2,128,128]{3,2,1,0:T(8,128)(2,1)}, u32[]{:S(2)}, u32[]{:S(2)}) collective-permute-start(bf16[5,2,128,128]{3,2,1,0:T(8,128)(2,1)S(1)} %get-tuple-element.28), channel_id=1, source_target_pairs={{0,3},{1,0},{2,1},{3,2},{4,7},{5,4},{6,5},{7,6},{8,11},{9,8},{10,9... | collective-permute-start | bytes 983048 | tf_op jit(solution)/shard_map/ppermute | solution.py:24
  52.0 14.5 %collective-permute-start.5 = (f32[2,128,128]{2,1,0:T(8,128)}, f32[2,128,128]{2,1,0:T(8,128)}, u32[]{:S(2)}, u32[]{:S(2)}) collective-permute-start(f32[2,128,128]{2,1,0:T(8,128)} %get-tuple-element.29), channel_id=1, source_target_pairs={{0,1},{1,2},{2,3},{3,0},{4,5},{5,6},{6,7},{7,4},{8,9},{9,10},{10,1... | collective-permute-start | bytes 393224 | tf_op jit(solution)/shard_map/ppermute | solution.py:24
  55.9 11.7 %collective-permute-start.6 = (f32[2,128,128]{2,1,0:T(8,128)}, f32[2,128,128]{2,1,0:T(8,128)}, u32[]{:S(2)}, u32[]{:S(2)}) collective-permute-start(f32[2,128,128]{2,1,0:T(8,128)} %get-tuple-element.30), channel_id=1, source_target_pairs={{0,3},{1,0},{2,1},{3,2},{4,7},{5,4},{6,5},{7,6},{8,11},{9,8},{10,9... | collective-permute-start | bytes 393224 | tf_op jit(solution)/shard_map/ppermute | solution.py:24
